TPU v7x, 128 devices: a whole 4x4x4 slice. The times are simulated.
128 devices in a mesh: child: 2 (over z_hi), row: 8 (over y, core), col: 8 (over x, z_lo).
Axes of the slice: x: 4, y: 4, z: 4 (z_hi: 2, z_lo: 2; z = z_hi * 2 + z_lo), core: 2. Of those that a mesh axis runs over, the one named last changes fastest.
Arguments:
- child_fronts: float32 [2, 8192, 8192], P('child', 'row', 'col')
- parent_front: float32 [12288, 12288], P('row', ('child', 'col')), may hold values from -6 to 6
- index_maps: int32 [2, 8192], replicated, may hold values from 0 to 12287, as said below
- orders: int32 [2], replicated, may hold values from 4096 to 8192, as said below
Outputs:
- assembled: float32 [12288, 12288], P('row', ('child', 'col'))
- panel_factor: float32 [2, 8192, 512], P('child', 'row')
Inputs may be any that keep to these rules, and one draw needn't show every extreme that they name: For each child, index_maps is one to one. Cut the child indices into aligned blocks of 8192 / 8 and the parent indices into 2 * 8 aligned slices of 12288 / (2 * 8): each block sends exactly 8192 / (2 * 8 * 8) of its indices into each slice. `orders`: one child's order is 8192.
All inputs are finite; a program needn't handle non-finite values.
Results may differ from a plain program's by a relative error of at most 0.0001.
Values sent between devices are 32-bit elements; how exact they have to be, the bound alone decides.
No kernel may reach another device: no remote copies, remote signals or barrier semaphores. Data moves between devices by JAX's collectives and lax.ppermute only.
A program may use at most 128 MiB of HBM per device.

v0:
```python
import jax
import jax.numpy as jnp
from jax import lax
from jax.sharding import PartitionSpec as P

PANEL = 512
FRONT = 8192


def from_root(value, axis, source):
    kept = jnp.where(lax.axis_index(axis) == source, value, 0).astype(value.dtype)
    return lax.psum(kept, axis)


def spread_sum(value, axis):
    count = lax.axis_size(axis)
    pieces = value.reshape(count, value.shape[0] // count, value.shape[1])
    arrived = lax.all_to_all(pieces, axis, 0, 0, tiled=True)
    return lax.all_gather(arrived.sum(0), axis, axis=0, tiled=True)


def from_first(value, axis):
    count = lax.axis_size(axis)
    pieces = value.reshape(count, value.shape[0] // count, value.shape[1])
    arrived = lax.all_to_all(pieces, axis, 0, 0, tiled=True)
    return lax.all_gather(arrived[0], axis, axis=0, tiled=True)


def select_rows(parent_map, owner, width, count):
    everywhere = jnp.arange(FRONT, dtype=jnp.int32)
    keyed = jnp.where(parent_map // width == owner, everywhere, everywhere + FRONT)
    chosen = jnp.argsort(keyed)[:count]
    return parent_map[chosen] - owner * width


def invert_slots(slots, length):
    count = slots.shape[0]
    lookup = jnp.full((length,), count, jnp.int32)
    return lookup.at[slots].set(jnp.arange(count, dtype=jnp.int32))


def one_hot(order, size):
    positions = jnp.arange(size, dtype=jnp.int32)
    return (positions[:, None] == order[None, :]).astype(jnp.float32)


def exact_matmul(values, select):
    return jnp.dot(values, select, precision=lax.Precision.HIGHEST)


def factor_and_invert(matrix, size):
    count = matrix.shape[0] // size
    eye = jnp.eye(size, dtype=jnp.float32)
    high = lax.Precision.HIGHEST
    trailing = (matrix + matrix.T) * 0.5
    factor, inverse = {}, {}
    for k in range(count):
        factor[k, k] = jnp.linalg.cholesky(trailing[:size, :size])
        inverse[k, k] = lax.linalg.triangular_solve(
            factor[k, k], eye, left_side=True, lower=True
        )
        if k + 1 < count:
            panel = jnp.dot(trailing[size:, :size], inverse[k, k].T, precision=high)
            for i in range(k + 1, count):
                factor[i, k] = panel[(i - k - 1) * size:(i - k) * size]
            trailing = trailing[size:, size:] - jnp.dot(panel, panel.T, precision=high)
    for i in range(count):
        for j in range(i - 1, -1, -1):
            total = sum(
                jnp.dot(factor[i, k], inverse[k, j], precision=high) for k in range(j, i)
            )
            inverse[i, j] = -jnp.dot(inverse[i, i], total, precision=high)
    zero = jnp.zeros((size, size), jnp.float32)

    def assemble(blocks):
        return jnp.concatenate(
            [
                jnp.concatenate(
                    [blocks[i, j] if j <= i else zero for j in range(count)], axis=1
                )
                for i in range(count)
            ]
        )

    return assemble(factor), assemble(inverse)


def factor_panel(diag_factor, inverse, columns, global_rows, own_order):
    solved = jnp.dot(columns, inverse.T, precision=lax.Precision.HIGHEST)
    top_rows = jnp.pad(diag_factor, ((0, columns.shape[0] - PANEL), (0, 0)))
    result = jnp.where(global_rows[:, None] < PANEL, top_rows, solved)
    return jnp.where(global_rows[:, None] < own_order, result, jnp.float32(0.0))


def on_device(child_fronts, parent_front, index_maps, orders):
    block_here = child_fronts[0]
    rows_here, cols_here = block_here.shape
    child_index = lax.axis_index("child")
    row_index = lax.axis_index("row")
    col_index = lax.axis_index("col")
    n_row = lax.axis_size("row")
    n_col = lax.axis_size("col")
    own_map = lax.dynamic_index_in_dim(index_maps, child_index, 0, keepdims=False)
    own_order = lax.dynamic_index_in_dim(orders, child_index, 0, keepdims=False)
    global_rows = row_index * rows_here + jnp.arange(rows_here, dtype=jnp.int32)
    global_cols = col_index * cols_here + jnp.arange(cols_here, dtype=jnp.int32)
    columns = from_first(block_here[:, :PANEL], "col")
    sent = jnp.concatenate(
        [
            jnp.where(row_index == col_index, columns, 0),
            jnp.where(row_index == 0, columns[:PANEL], 0),
        ]
    )
    received = spread_sum(sent, "row")
    other_columns, corner = received[:rows_here], received[rows_here:]
    parent_rows, parent_cols = parent_front.shape
    row_map = lax.dynamic_slice_in_dim(own_map, row_index * rows_here, rows_here)
    col_map = lax.dynamic_slice_in_dim(own_map, col_index * cols_here, cols_here)
    row_keys = row_map // parent_rows * rows_here + jnp.arange(rows_here, dtype=jnp.int32)
    col_keys = col_map // parent_cols * cols_here + jnp.arange(cols_here, dtype=jnp.int32)
    col_order = jnp.argsort(col_keys)
    row_order = jnp.argsort(row_keys)
    turned_block = jnp.einsum(
        "qj,iq->ji", one_hot(col_order, cols_here), block_here[row_order],
        precision=lax.Precision.HIGHEST,
    )
    diag_factor, inverse = factor_and_invert(corner, PANEL // 4)
    own_panel = factor_panel(diag_factor, inverse, columns, global_rows, own_order)
    high = lax.Precision.HIGHEST
    turned_panels = jnp.dot(
        jnp.dot(other_columns[col_order], inverse.T, precision=high),
        jnp.dot(columns[row_order], inverse.T, precision=high).T,
        precision=high,
    )
    live_rows = (global_rows >= PANEL) & (global_rows < own_order)
    live_cols = (global_cols >= PANEL) & (global_cols < own_order)
    turned = jnp.where(
        live_cols[col_order][:, None] & live_rows[row_order][None, :],
        turned_block - turned_panels,
        jnp.float32(0.0),
    )
    part_rows = rows_here // n_row
    part_cols = cols_here // (2 * n_col)
    pieces = (
        turned.reshape(2, n_col, part_cols, n_row, part_rows)
        .transpose(0, 3, 1, 2, 4)
        .reshape(-1, part_rows)
    )
    arrived = lax.all_to_all(
        pieces, ("child", "row", "col"), split_axis=0, concat_axis=0, tiled=True
    )
    arrived = (
        arrived.reshape(2, n_row, n_col, part_cols, part_rows)
        .transpose(0, 2, 3, 1, 4)
        .reshape(2, n_col * part_cols, rows_here)
    )
    col_owner = child_index * n_col + col_index
    assembled = parent_front
    for source in range(2):
        parent_map = index_maps[source]
        row_slots = select_rows(parent_map, row_index, parent_rows, rows_here)
        col_slots = select_rows(parent_map, col_owner, parent_cols, n_col * part_cols)
        row_lookup = invert_slots(row_slots, parent_rows)
        spread = jnp.einsum(
            "qi,pq->ip", arrived[source], one_hot(col_slots, parent_cols),
            precision=lax.Precision.HIGHEST,
        )
        padded = jnp.pad(spread, ((0, 1), (0, 0)))
        assembled = assembled + jnp.take(padded, row_lookup, axis=0)
    return (assembled, own_panel[None])


def solution(mesh):
    in_specs = (P("child", "row", "col"), P("row", ("child", "col")), P(), P())
    out_specs = (P("row", ("child", "col")), P("child", "row", None))
    return jax.shard_map(
        on_device, mesh=mesh, in_specs=in_specs, out_specs=out_specs, check_vma=False
    )
```

profile of v0, /device:TPU:0, one launch (start us, length us, event | category | flops | bytes accessed | tf_op | source)
XLA Modules:
  0.0 480.5 jit_solution(12069542778287017059)
XLA Ops:
  7.2 1.8 slice.139
  9.0 32.2 %all_to_all.19 = f32[8,128,512]{2,1,0:T(8,128)S(1)} all-to-all(f32[8,128,512]{2,1,0:T(8,128)S(1)} %bitcast.143), channel_id=1, replica_groups=mesh['child'=2,'row'=8,'col'=8] {'col'}, dimensions={0} | all-to-all | bytes 4194304 | tf_op jit(solution)/shard_map/all_to_all | solution.py:25
  41.1 0.7 slice.140
  42.0 52.0 %all-gather.6.cloned.1.call-done = f32[1,1024,512]{2,1,0:T(8,128)} async-done(((f32[1,128,512]{2,1,0:T(8,128)}), f32[1,1024,512]{2,1,0:T(8,128)}) %all-gather.6.cloned.1.call-update) | async-done | bytes 2097168 | tf_op jit(solution)/shard_map/all_gather | solution.py:26
  93.9 1.5 fusion.18
  96.4 42.6 %all_to_all.20 = f32[8,192,512]{2,1,0:T(8,128)} all-to-all(f32[8,192,512]{2,1,0:T(8,128)S(1)} %bitcast.142), channel_id=1, replica_groups=mesh['child'=2,'row'=8,'col'=8] {'row'}, dimensions={0} | all-to-all | bytes 6291456 | tf_op jit(solution)/shard_map/all_to_all | solution.py:18
  139.0 3.0 reduce_sum.9
  143.0 4.4 sort.91
  147.4 8.5 %gather_fusion.2 = f32[1024,1024]{1,0:T(8,128)} fusion(f32[1024,1024]{1,0:T(8,128)} %bitcast.135, s32[1024]{0:T(1024)S(1)} %fusion.59), kind=kCustom, calls=%fused_computation.4 | custom fusion | bytes 8392704 | tf_op jit(solution)/shard_map/gather | solution.py:124
  156.5 11.0 %gather_fusion.1 = pred[1024]{0:T(1024)(128)(4,1)} fusion(pred[1024]{0:T(1024)(128)(4,1)S(1)} %get-tuple-element.49, s32[1024]{0:T(1024)S(1)} %fusion.59), kind=kCustom, calls=%fused_computation.3 | custom fusion | bytes 6144 | tf_op jit(solution)/shard_map/gather | solution.py:138
  168.3 6.8 %sort.95 = (s32[8192]{0:T(1024)}, s32[8192]{0:T(1024)S(1)}) sort(s32[8192]{0:T(1024)S(1)} %get-tuple-element.40, s32[8192]{0:T(1024)S(1)} %iota.139), dimensions={0}, to_apply=%region_9.13 | sort | flops 106496 | bytes 131072 | tf_op jit(solution)/shard_map/jit(argsort)/sort | solution.py:32
  175.0 6.1 %gather_fusion.8 = s32[1024]{0:T(1024)S(1)} fusion(s32[8192]{0:T(1024)S(1)} %bitcast.132, s32[1024]{0:T(1024)S(1)} %fusion.61), kind=kCustom, calls=%fused_computation.10 | custom fusion | bytes 12288 | tf_op jit(solution)/shard_map/gather | solution.py:33
  181.2 6.8 %sort.94 = (s32[8192]{0:T(1024)}, s32[8192]{0:T(1024)S(1)}) sort(s32[8192]{0:T(1024)S(1)} %get-tuple-element.41, s32[8192]{0:T(1024)S(1)} %iota.137), dimensions={0}, to_apply=%region_8.12 | sort | flops 106496 | bytes 131072 | tf_op jit(solution)/shard_map/jit(argsort)/sort | solution.py:32
  188.0 3.1 gather_fusion.7
  191.1 4.4 sort.90
  195.5 11.2 %gather_fusion = pred[1024]{0:T(1024)(128)(4,1)} fusion(pred[1024]{0:T(1024)(128)(4,1)S(1)} %get-tuple-element.48, s32[1024]{0:T(1024)S(1)} %fusion.58), kind=kCustom, calls=%fused_computation.2 | custom fusion | bytes 6144 | tf_op jit(solution)/shard_map/gather | solution.py:138
  206.7 6.8 %sort.92 = (s32[8192]{0:T(1024)}, s32[8192]{0:T(1024)}) sort(s32[8192]{0:T(1024)S(1)} %get-tuple-element.42, s32[8192]{0:T(1024)S(1)} %iota.132), dimensions={0}, to_apply=%region_5.8 | sort | flops 106496 | bytes 131072 | tf_op jit(solution)/shard_map/jit(argsort)/sort | solution.py:32
  213.5 11.4 %fusion.1 = f32[1024,1024]{1,0:T(8,128)} fusion(f32[1024,1024]{1,0:T(8,128)} %gather_fusion.2, s32[1024]{0:T(1024)S(1)} %get-tuple-element.11), kind=kOutput, calls=%fused_computation.20 | convolution fusion | flops 12886999040 | bytes 8392704 | tf_op jit(solution)/shard_map/qj,iq->ji/dot_general | solution.py:123
  224.9 5.3 %gather_fusion.4 = f32[1024,512]{1,0:T(8,128)} fusion(f32[1024,512]{1,0:T(8,128)S(1)} %bitcast.136, s32[1024]{0:T(1024)S(1)} %fusion.59), kind=kCustom, calls=%fused_computation.6 | custom fusion | bytes 4198400 | tf_op jit(solution)/shard_map/gather | solution.py:132
  230.2 1.2 slice-done
  231.4 1.3 copy.30
  232.7 1.8 fusion.19
  234.6 11.7 %cholesky.74 = f32[128,128]{1,0:T(8,128)S(1)} custom-call(f32[128,128]{1,0:T(8,128)S(1)} %fusion.43), custom_call_target="Cholesky" | custom-call | tf_op jit(solution)/shard_map/jit(cholesky)/cholesky | solution.py:58
  247.0 1.3 select_bitcast_fusion.4
  248.3 9.8 %custom-call.8 = f32[1,128,128]{1,2,0:T(8,128)S(1)} custom-call(f32[1,128,128]{2,1,0:T(8,128)S(1)} %get-tuple-element.25), custom_call_target="InvertDiagBlocksLowerTriangular" | custom-call | tf_op jit(solution)/shard_map/triangular_solve/custom-call.0 | solution.py:59
  260.4 0.9 fusion.41
  261.3 11.7 %cholesky.85 = f32[128,128]{1,0:T(8,128)S(1)} custom-call(f32[128,128]{1,0:T(8,128)S(1)} %fusion.41), custom_call_target="Cholesky" | custom-call | tf_op jit(solution)/shard_map/jit(cholesky)/cholesky | solution.py:58
  273.8 1.3 select_bitcast_fusion.3
  275.1 9.8 %custom-call.9 = f32[1,128,128]{1,2,0:T(8,128)S(1)} custom-call(f32[1,128,128]{2,1,0:T(8,128)S(1)} %get-tuple-element.23), custom_call_target="InvertDiagBlocksLowerTriangular" | custom-call | tf_op jit(solution)/shard_map/triangular_solve/custom-call.0 | solution.py:59
  285.9 1.2 fusion.32
  287.1 1.4 convolution_subtract_fusion.1
  288.6 11.7 %cholesky.96 = f32[128,128]{1,0:T(8,128)S(1)} custom-call(f32[128,128]{1,0:T(8,128)S(1)} %fusion.39), custom_call_target="Cholesky" | custom-call | tf_op jit(solution)/shard_map/jit(cholesky)/cholesky | solution.py:58
  301.0 1.3 select_bitcast_fusion.2
  302.3 9.8 %custom-call.10 = f32[1,128,128]{1,2,0:T(8,128)S(1)} custom-call(f32[1,128,128]{2,1,0:T(8,128)S(1)} %get-tuple-element.21), custom_call_target="InvertDiagBlocksLowerTriangular" | custom-call | tf_op jit(solution)/shard_map/triangular_solve/custom-call.0 | solution.py:59
  314.6 3.1 slice.142
  317.7 7.0 %gather_fusion.3 = f32[1024,512]{1,0:T(8,128)} fusion(f32[1024,512]{1,0:T(8,128)} %slice.142, s32[1024]{0:T(1024)S(1)} %fusion.58), kind=kCustom, calls=%fused_computation.5 | custom fusion | bytes 4198400 | tf_op jit(solution)/shard_map/gather | solution.py:131
  326.0 11.7 %cholesky.107 = f32[128,128]{1,0:T(8,128)S(1)} custom-call(f32[128,128]{1,0:T(8,128)S(1)} %fusion.37), custom_call_target="Cholesky" | custom-call | tf_op jit(solution)/shard_map/jit(cholesky)/cholesky | solution.py:58
  338.4 1.3 select_bitcast_fusion.1
  339.7 9.8 %custom-call.11 = f32[1,128,128]{1,2,0:T(8,128)S(1)} custom-call(f32[1,128,128]{2,1,0:T(8,128)S(1)} %get-tuple-element.19), custom_call_target="InvertDiagBlocksLowerTriangular" | custom-call | tf_op jit(solution)/shard_map/triangular_solve/custom-call.0 | solution.py:59
  351.7 5.2 %fusion.89 = f32[1024,512]{1,0:T(8,128)S(1)} fusion(f32[1024,512]{1,0:T(8,128)} %gather_fusion.3, f32[128,256]{1,0:T(8,128)S(1)} %broadcast.165, f32[128,128]{1,0:T(8,128)S(1)} %cholesky.75, f32[128,128]{1,0:T(8,128)S(1)} %fusion.30, f32[128,128]{1,0:T(8,128)S(1)} %copy.51, f32[128,128]{1,0:T(8,128)S(1)} %convolution_negate_fusion, ...), kind=kOutput, calls=%fused_computation.192 | convolution fusion | flops 3224633344 | bytes 5046272 | tf_op jit(solution)/shard_map/dot_general | solution.py:131
  357.1 3.9 fusion.87
  361.0 7.0 %select_bitcast_fusion = f32[128,8,8,128]{3,1,2,0:T(8,128)S(1)} fusion(f32[1024,1024]{1,0:T(8,128)S(1)} %copy-done.1, f32[1024,512]{1,0:T(8,128)S(1)} %fusion.89, f32[1024,512]{1,0:T(8,128)S(1)} %fusion.87, pred[1024]{0:T(1024)(128)(4,1)S(1)} %copy-done.18, pred[1024]{0:T(1024)(128)(4,1)S(1)} %copy-done.19), kind=kOutput, calls=%fused_computation.16 | convolution fusion | flops 6445596672 | bytes 12584960 | tf_op jit(solution)/shard_map/dot_general | solution.py:130
  368.0 1.0 copy.71
  369.0 3.0 copy.52
  372.0 8.0 %all-to-all-start.2 = ((f32[128,64,128]{2,1,0:T(8,128)}), f32[128,64,128]{2,1,0:T(8,128)}, u32[]{:S(2)}, u32[]{:S(2)}) async-start(f32[128,64,128]{2,1,0:T(8,128)} %bitcast.137), calls=%async_computation.2 | async-start | bytes 8388608 | tf_op jit(solution)/shard_map/all_to_all | solution.py:149
  380.7 3.1 gather_fusion.5
  383.9 6.8 %sort.93 = (s32[8192]{0:T(1024)}, s32[8192]{0:T(1024)S(1)}) sort(s32[8192]{0:T(1024)S(1)} %copy-done.7, s32[8192]{0:T(1024)S(1)} %iota.134), dimensions={0}, to_apply=%region_6.9 | sort | flops 106496 | bytes 131072 | tf_op jit(solution)/shard_map/jit(argsort)/sort | solution.py:32
  390.6 6.1 %gather_fusion.6 = s32[1024]{0:T(1024)S(1)} fusion(s32[8192]{0:T(1024)S(1)} %bitcast.130, s32[1024]{0:T(1024)S(1)} %fusion.60), kind=kCustom, calls=%fused_computation.8 | custom fusion | bytes 12288 | tf_op jit(solution)/shard_map/gather | solution.py:33
  396.8 4.3 scatter_custom_fusion.1
  401.2 4.5 scatter_custom_fusion
  405.7 1.2 fusion.66
  408.8 0.7 copy.54
  409.5 0.7 copy.66
  411.7 0.7 copy.68
  413.1 1.2 fusion.17
  414.4 6.0 %fusion.10 = f32[1,1024,512]{2,1,0:T(8,128)} fusion(f32[512,512]{1,0:T(8,128)S(1)} %fusion.17, pred[1024]{0:T(1024)(128)(4,1)} %get-tuple-element.44, pred[1024]{0:T(1024)(128)(4,1)} %get-tuple-element.45, f32[1,1024,512]{2,1,0:T(8,128)S(1)} %copy-done, f32[128,256]{1,0:T(8,128)S(1)} %broadcast.165, f32[128,128]{1,0:T(8,128)} %copy-done.6, ...), kind=kOutput, calls=%fused_computation.29 | convolution fusion | flops 3225681920 | bytes 6096896 | tf_op jit(solution)/shard_map/dot_general | solution.py:89
  420.4 11.6 %all-to-all-done.2 = f32[128,64,128]{2,1,0:T(8,128)} async-done(((f32[128,64,128]{2,1,0:T(8,128)}), f32[128,64,128]{2,1,0:T(8,128)}, u32[]{:S(2)}, u32[]{:S(2)}) %all-to-all-start.2) | async-done | bytes 4194336 | tf_op jit(solution)/shard_map/all_to_all | solution.py:149
  432.0 5.5 %copy.83 = f32[2,8,8,64,128]{4,1,3,2,0:T(8,128)S(1)} copy(f32[2,8,8,64,128]{4,3,2,1,0:T(8,128)} %bitcast.26) | data formatting | bytes 8388608 | tf_op jit(solution)/shard_map/reshape | solution.py:153
  437.8 5.5 %fusion.3 = f32[1024,768]{1,0:T(8,128)S(1)} fusion(f32[64,8,8,128]{3,2,1,0:T(8,128)S(1)} %bitcast.141, s32[512]{0:T(512)S(1)} %broadcast_subtract_fusion.2), kind=kOutput, calls=%fused_computation.21 | convolution fusion | flops 4832231424 | bytes 5244928 | tf_op jit(solution)/shard_map/qi,pq->ip/dot_general | solution.py:164
  444.0 5.2 %fusion.6 = f32[1024,768]{1,0:T(8,128)S(1)} fusion(f32[64,8,8,128]{3,2,1,0:T(8,128)S(1)} %bitcast.140, s32[512]{0:T(512)S(1)} %copy-done.17), kind=kOutput, calls=%fused_computation.24 | convolution fusion | flops 4832231424 | bytes 5244928 | tf_op jit(solution)/shard_map/qi,pq->ip/dot_general | solution.py:164
  449.2 1.9 pad.13
  451.1 8.6 %gather_fusion.9 = f32[1536,768]{1,0:T(8,128)} fusion(f32[1025,768]{1,0:T(8,128)} %pad.13, s32[2048]{0:T(1024)S(1)} %copy-done.15), kind=kCustom, calls=%fused_computation.clone | custom fusion | bytes 9443328 | tf_op jit(solution)/shard_map/jit(_take)/gather | solution.py:169
  459.8 5.5 %gather_fusion.10 = f32[1536,768]{1,0:T(8,128)} fusion(f32[1025,768]{1,0:T(8,128)S(1)} %pad.14, s32[2048]{0:T(1024)S(1)} %pad_clamp_fusion), kind=kCustom, calls=%fused_computation.1.clone | custom fusion | bytes 9443328 | tf_op jit(solution)/shard_map/jit(_take)/gather | solution.py:169
  465.3 8.0 %select_add_fusion = f32[1536,768]{1,0:T(8,128)} fusion(f32[1536,768]{1,0:T(8,128)} %gather_fusion.10, f32[1536,768]{1,0:T(8,128)} %param.10, f32[1536,768]{1,0:T(8,128)} %gather_fusion.9, pred[1536]{0:T(1024)(128)(4,1)S(1)} %compare_and_fusion, pred[1536]{0:T(1024)(128)(4,1)S(1)} %copy-done.16), kind=kLoop, calls=%fused_computation.13 | loop fusion | flops 4718592 | bytes 18877440 | tf_op jit(solution)/shard_map/add | solution.py:169
  (139 shorter events, 21.3 us)
Async XLA Ops:
  7.2 86.7 %all-gather.6.cloned.1.call-start = ((), (), s32[]{:S(2)}) async-start(), calls=%async_computation.4 | async-start | bytes 2359296 | tf_op jit(solution)/shard_map/all_gather | solution.py:26
  41.9 188.3 %all-gather.4.cloned.1.call-start = ((), (), s32[]{:S(2)}) async-start(), calls=%async_computation.3 | async-start | bytes 3538944 | tf_op jit(solution)/shard_map/all_gather | solution.py:19
  93.9 1.9 copy-start
  139.0 3.1 copy-start.20
  139.0 3.7 copy-start.8
  230.2 1.2 slice-start
  259.4 0.9 copy-start.2
  349.8 7.1 %copy-start.14 = (f32[128,128]{1,0:T(8,128)}, f32[128,128]{1,0:T(8,128)S(1)}, u32[]{:S(2)}) copy-start(f32[128,128]{1,0:T(8,128)S(1)} %copy.51) | copy-start | bytes 196612
  350.4 6.5 %copy-start.9 = (f32[128,128]{1,0:T(8,128)}, f32[128,128]{1,0:T(8,128)S(1)}, u32[]{:S(2)}) copy-start(f32[128,128]{1,0:T(8,128)S(1)} %convolution_negate_fusion.2) | copy-start | bytes 196612
  350.7 6.2 %copy-start.10 = (f32[128,128]{1,0:T(8,128)}, f32[128,128]{1,0:T(8,128)S(1)}, u32[]{:S(2)}) copy-start(f32[128,128]{1,0:T(8,128)S(1)} %convolution_negate_fusion) | copy-start | bytes 196612
  351.0 5.9 %copy-start.4 = (f32[128,128]{1,0:T(8,128)}, f32[128,128]{1,0:T(8,128)S(1)}, u32[]{:S(2)}) copy-start(f32[128,128]{1,0:T(8,128)S(1)} %convolution_negate_fusion.3) | copy-start | bytes 196612
  351.6 5.3 %copy-start.11 = (f32[128,128]{1,0:T(8,128)}, f32[128,128]{1,0:T(8,128)S(1)}, u32[]{:S(2)}) copy-start(f32[128,128]{1,0:T(8,128)S(1)} %convolution_negate_fusion.1) | copy-start | bytes 196612
  351.7 5.3 %copy-start.6 = (f32[128,128]{1,0:T(8,128)}, f32[128,128]{1,0:T(8,128)S(1)}, u32[]{:S(2)}) copy-start(f32[128,128]{1,0:T(8,128)S(1)} %cholesky.75) | copy-start | bytes 196612
  351.7 5.3 %copy-start.3 = (f32[1024,512]{1,0:T(8,128)S(1)}, f32[1024,512]{1,0:T(8,128)}, u32[]{:S(2)}) copy-start(f32[1024,512]{1,0:T(8,128)} %gather_fusion.4) | copy-start | bytes 6291460
  351.7 5.3 %copy-start.12 = (f32[128,128]{1,0:T(8,128)S(1)}, f32[128,128]{1,0:T(8,128)}, u32[]{:S(2)}) copy-start(f32[128,128]{1,0:T(8,128)} %copy.36) | copy-start | bytes 196612
  351.7 5.3 %copy-start.13 = (f32[128,128]{1,0:T(8,128)S(1)}, f32[128,128]{1,0:T(8,128)}, u32[]{:S(2)}) copy-start(f32[128,128]{1,0:T(8,128)} %copy.43) | copy-start | bytes 196612
  357.0 3.9 copy-start.1
  357.0 3.9 copy-start.18
  357.1 3.9 copy-start.19
  372.0 60.0 %all-to-all-start.2 = ((f32[128,64,128]{2,1,0:T(8,128)}), f32[128,64,128]{2,1,0:T(8,128)}, u32[]{:S(2)}, u32[]{:S(2)}) async-start(f32[128,64,128]{2,1,0:T(8,128)} %bitcast.137), calls=%async_computation.2 | async-start | bytes 8388608 | tf_op jit(solution)/shard_map/all_to_all | solution.py:149
  380.0 3.9 copy-start.7
  396.8 17.6 %copy-start.5 = (f32[128,128]{1,0:T(8,128)S(1)}, f32[128,128]{1,0:T(8,128)}, u32[]{:S(2)}) copy-start(f32[128,128]{1,0:T(8,128)} %copy-done.4) | copy-start | bytes 196612
  443.3 0.7 copy-start.17
  449.2 1.9 copy-start.15
  459.8 5.5 %copy-start.16 = (pred[1536]{0:T(1024)(128)(4,1)S(1)}, pred[1536]{0:T(1024)(128)(4,1)}, u32[]{:S(2)}) copy-start(pred[1536]{0:T(1024)(128)(4,1)} %compare_and_fusion.1) | copy-start | bytes 4612
Sparse Core Ops, SparseCore 0:
  42.0 51.8 all-gather.5
  142.2 26.5 all-gather.3
where the time goes:
time: 490 us; the launch traced here: 481 us
  other arithmetic  152 us (31%)
  local copies, waits for them, and re-layouts  112 us (23%)
  blocking collectives  74.8 us (15%)
  waiting for transfers between devices  63.6 us (13%)
  matrix products  54 us (11%)
  between operations  15.5 us (3%)
  starting transfers between devices  8.06 us (2%)
    all_gather x1, waiting for transfers between devices, from_first(): return lax.all_gather(arrived[0], axis, axis=0, tiled=True)  52 us
    another operation x12, other arithmetic, factor_and_invert(): factor[k, k] = jnp.linalg.cholesky(trailing[:size, :size])  49.7 us
    another operation x8, other arithmetic, factor_and_invert(): lax.linalg.triangular_solve(factor[k, k], eye, left_side=True, lower=True)  44.3 us
    all_to_all x1, blocking collectives, spread_sum(): arrived = lax.all_to_all(pieces, axis, 0, 0, tiled=True)  42.6 us
    all_to_all x1, blocking collectives, from_first(): arrived = lax.all_to_all(pieces, axis, 0, 0, tiled=True)  32.2 us
    sort x4, other arithmetic, select_rows(): chosen = jnp.argsort(keyed)[:count]  27 us
    gather x4, local copies, waits for them, and re-layouts, select_rows(): return parent_map[chosen] - owner * width  18.6 us
    gather x2, local copies, waits for them, and re-layouts, on_device(): assembled = assembled + jnp.take(padded, row_lookup, axis=0)  14.1 us
  transfers between devices with their start and end apart: 3, of which 2 were waited for; matrix products, arithmetic and copies ran while one was open for 27% of the time, Pallas kernels for 0%

commit v1 on v0

--- a/solution.py
+++ b/solution.py
@@ -105,14 +105,6 @@
     global_rows = row_index * rows_here + jnp.arange(rows_here, dtype=jnp.int32)
     global_cols = col_index * cols_here + jnp.arange(cols_here, dtype=jnp.int32)
     columns = from_first(block_here[:, :PANEL], "col")
-    sent = jnp.concatenate(
-        [
-            jnp.where(row_index == col_index, columns, 0),
-            jnp.where(row_index == 0, columns[:PANEL], 0),
-        ]
-    )
-    received = spread_sum(sent, "row")
-    other_columns, corner = received[:rows_here], received[rows_here:]
     parent_rows, parent_cols = parent_front.shape
     row_map = lax.dynamic_slice_in_dim(own_map, row_index * rows_here, rows_here)
     col_map = lax.dynamic_slice_in_dim(own_map, col_index * cols_here, cols_here)
@@ -124,7 +116,19 @@
         "qj,iq->ji", one_hot(col_order, cols_here), block_here[row_order],
         precision=lax.Precision.HIGHEST,
     )
+    sent = jnp.concatenate(
+        [
+            jnp.where(row_index == col_index, columns, 0),
+            jnp.where(row_index == 0, columns[:PANEL], 0),
+        ]
+    )
+    sent, row_order, col_order, turned_block = lax.optimization_barrier(
+        (sent, row_order, col_order, turned_block)
+    )
+    received = spread_sum(sent, "row")
+    other_columns, corner = received[:rows_here], received[rows_here:]
     diag_factor, inverse = factor_and_invert(corner, PANEL // 4)
+    late_maps, diag_factor = lax.optimization_barrier((index_maps, diag_factor))
     own_panel = factor_panel(diag_factor, inverse, columns, global_rows, own_order)
     high = lax.Precision.HIGHEST
     turned_panels = jnp.dot(
@@ -157,7 +161,7 @@
     col_owner = child_index * n_col + col_index
     assembled = parent_front
     for source in range(2):
-        parent_map = index_maps[source]
+        parent_map = late_maps[source]
         row_slots = select_rows(parent_map, row_index, parent_rows, rows_here)
         col_slots = select_rows(parent_map, col_owner, parent_cols, n_col * part_cols)
         row_lookup = invert_slots(row_slots, parent_rows)

time: 490 us -> 447 us (0.912)
  waiting for transfers between devices: 63.6 us -> 27 us
  local copies, waits for them, and re-layouts: 112 us -> 102 us
  other arithmetic: 152 us -> 157 us
    all_gather x1, waiting for transfers between devices: 52 us -> 21.4 us  [from_first(): return lax.all_gather(arrived[0], axis, axis=0, tiled=True)]
    all_to_all x1, waiting for transfers between devices: 11.6 us -> 0.01 us  [on_device(): lax.all_to_all(pieces, ('child', 'row', 'col'), split_axis=0, concat_axis...]
    all_gather x1, waiting for transfers between devices: 0.02 us -> 5.55 us  [spread_sum(): return lax.all_gather(arrived.sum(0), axis, axis=0, tiled=True)]
where the time goes in v1:
time: 447 us; the launch traced here: 439 us
  other arithmetic  157 us (35%)
  local copies, waits for them, and re-layouts  102 us (23%)
  blocking collectives  74.8 us (17%)
  matrix products  53.9 us (12%)
  waiting for transfers between devices  27 us (6%)
  between operations  15.2 us (3%)
  starting transfers between devices  9.3 us (2%)
    another operation x12, other arithmetic, factor_and_invert(): factor[k, k] = jnp.linalg.cholesky(trailing[:size, :size])  50.1 us
    another operation x8, other arithmetic, factor_and_invert(): lax.linalg.triangular_solve(factor[k, k], eye, left_side=True, lower=True)  44.7 us
    all_to_all x1, blocking collectives, spread_sum(): arrived = lax.all_to_all(pieces, axis, 0, 0, tiled=True)  42.7 us
    all_to_all x1, blocking collectives, from_first(): arrived = lax.all_to_all(pieces, axis, 0, 0, tiled=True)  32.2 us
    sort x4, other arithmetic, select_rows(): chosen = jnp.argsort(keyed)[:count]  27.9 us
    all_gather x1, waiting for transfers between devices, from_first(): return lax.all_gather(arrived[0], axis, axis=0, tiled=True)  21.4 us
    gather x4, local copies, waits for them, and re-layouts, select_rows(): return parent_map[chosen] - owner * width  19.9 us
    gather x2, local copies, waits for them, and re-layouts, on_device(): assembled = assembled + jnp.take(padded, row_lookup, axis=0)  14.2 us
  transfers between devices with their start and end apart: 3, of which 2 were waited for; matrix products, arithmetic and copies ran while one was open for 27% of the time, Pallas kernels for 0%

profile of v1, /device:TPU:0, one launch (start us, length us, event | category | flops | bytes accessed | tf_op | source)
XLA Modules:
  0.0 439.4 jit_solution(13483453451293392631)
XLA Ops:
  7.2 1.8 slice.139
  9.0 32.2 %all_to_all.19 = f32[8,128,512]{2,1,0:T(8,128)S(1)} all-to-all(f32[8,128,512]{2,1,0:T(8,128)S(1)} %bitcast.141), channel_id=1, replica_groups=mesh['child'=2,'row'=8,'col'=8] {'col'}, dimensions={0} | all-to-all | bytes 4194304 | tf_op jit(solution)/shard_map/all_to_all | solution.py:25
  41.1 0.7 slice.140
  42.0 0.9 and_reduce_fusion
  42.9 0.9 broadcast_divide_fusion
  43.8 4.4 sort.90
  48.2 8.5 %gather_fusion = f32[1024,1024]{1,0:T(8,128)} fusion(f32[1024,1024]{1,0:T(8,128)} %bitcast.133, s32[1024]{0:T(1024)S(1)} %fusion.57), kind=kCustom, calls=%fused_computation.2 | custom fusion | bytes 8392704 | tf_op jit(solution)/shard_map/gather | solution.py:116
  56.7 4.4 sort.91
  61.1 11.4 %fusion.1 = f32[1024,1024]{1,0:T(8,128)} fusion(f32[1024,1024]{1,0:T(8,128)} %gather_fusion, s32[1024]{0:T(1024)S(1)} %get-tuple-element.19), kind=kOutput, calls=%fused_computation.20 | convolution fusion | flops 12886999040 | bytes 8392704 | tf_op jit(solution)/shard_map/qj,iq->ji/dot_general | solution.py:115
  72.5 21.4 %all-gather.6.cloned.1.call-done = f32[1,1024,512]{2,1,0:T(8,128)} async-done(((f32[1,128,512]{2,1,0:T(8,128)}), f32[1,1024,512]{2,1,0:T(8,128)}) %all-gather.6.cloned.1.call-update) | async-done | bytes 2097168 | tf_op jit(solution)/shard_map/all_gather | solution.py:26
  93.9 2.0 broadcast_select_fusion
  96.5 42.7 %all_to_all.20 = f32[8,192,512]{2,1,0:T(8,128)} all-to-all(f32[8,192,512]{2,1,0:T(8,128)S(1)} %bitcast.140), channel_id=1, replica_groups=mesh['child'=2,'row'=8,'col'=8] {'row'}, dimensions={0} | all-to-all | bytes 6291456 | tf_op jit(solution)/shard_map/all_to_all | solution.py:18
  139.2 3.0 reduce_sum.9
  142.8 1.2 fusion.66
  144.7 4.9 %gather_fusion.4 = f32[1024,512]{1,0:T(8,128)} fusion(f32[1024,512]{1,0:T(8,128)S(1)} %bitcast.134, s32[1024]{0:T(1024)S(1)} %get-tuple-element.59), kind=kCustom, calls=%fused_computation.6 | custom fusion | bytes 4198400 | tf_op jit(solution)/shard_map/gather | solution.py:136
  149.6 6.8 %gather_fusion.2 = pred[1024]{0:T(1024)(128)(4,1)S(1)} fusion(pred[1024]{0:T(1024)(128)(4,1)S(1)} %get-tuple-element.61, s32[1024]{0:T(1024)S(1)} %get-tuple-element.59), kind=kCustom, calls=%fused_computation.4 | custom fusion | bytes 6144 | tf_op jit(solution)/shard_map/gather | solution.py:142
  156.4 7.0 %gather_fusion.1 = pred[1024]{0:T(1024)(128)(4,1)S(1)} fusion(pred[1024]{0:T(1024)(128)(4,1)S(1)} %get-tuple-element.60, s32[1024]{0:T(1024)S(1)} %get-tuple-element.58), kind=kCustom, calls=%fused_computation.3 | custom fusion | bytes 6144 | tf_op jit(solution)/shard_map/gather | solution.py:142
  163.4 5.5 %all-gather.4.cloned.1.call-done = f32[1536,512]{1,0:T(8,128)} async-done(((f32[192,512]{1,0:T(8,128)}), f32[1536,512]{1,0:T(8,128)}) %all-gather.4.cloned.1.call-update) | async-done | bytes 3145744 | tf_op jit(solution)/shard_map/all_gather | solution.py:19
  168.9 1.2 slice-done
  170.1 1.3 copy.30
  171.4 1.8 fusion.19
  173.4 11.7 %cholesky.74 = f32[128,128]{1,0:T(8,128)S(1)} custom-call(f32[128,128]{1,0:T(8,128)S(1)} %fusion.43), custom_call_target="Cholesky" | custom-call | tf_op jit(solution)/shard_map/jit(cholesky)/cholesky | solution.py:58
  186.4 9.8 %custom-call.8 = f32[1,128,128]{1,2,0:T(8,128)S(1)} custom-call(f32[1,128,128]{2,1,0:T(8,128)S(1)} %get-tuple-element.37), custom_call_target="InvertDiagBlocksLowerTriangular" | custom-call | tf_op jit(solution)/shard_map/triangular_solve/custom-call.0 | solution.py:59
  197.5 0.8 copy-done.2
  198.4 0.9 fusion.41
  199.3 11.7 %cholesky.85 = f32[128,128]{1,0:T(8,128)S(1)} custom-call(f32[128,128]{1,0:T(8,128)S(1)} %fusion.41), custom_call_target="Cholesky" | custom-call | tf_op jit(solution)/shard_map/jit(cholesky)/cholesky | solution.py:58
  211.7 1.3 select_bitcast_fusion.3
  213.0 10.0 %custom-call.9 = f32[1,128,128]{1,2,0:T(8,128)S(1)} custom-call(f32[1,128,128]{2,1,0:T(8,128)S(1)} %get-tuple-element.35), custom_call_target="InvertDiagBlocksLowerTriangular" | custom-call | tf_op jit(solution)/shard_map/triangular_solve/custom-call.0 | solution.py:59
  223.2 1.2 fusion.32
  224.5 1.4 convolution_subtract_fusion.1
  226.0 11.7 %cholesky.96 = f32[128,128]{1,0:T(8,128)S(1)} custom-call(f32[128,128]{1,0:T(8,128)S(1)} %fusion.39), custom_call_target="Cholesky" | custom-call | tf_op jit(solution)/shard_map/jit(cholesky)/cholesky | solution.py:58
  238.4 1.3 select_bitcast_fusion.2
  239.7 9.8 %custom-call.10 = f32[1,128,128]{1,2,0:T(8,128)S(1)} custom-call(f32[1,128,128]{2,1,0:T(8,128)S(1)} %get-tuple-element.33), custom_call_target="InvertDiagBlocksLowerTriangular" | custom-call | tf_op jit(solution)/shard_map/triangular_solve/custom-call.0 | solution.py:59
  254.4 12.1 %cholesky.107 = f32[128,128]{1,0:T(8,128)S(1)} custom-call(f32[128,128]{1,0:T(8,128)S(1)} %fusion.37), custom_call_target="Cholesky" | custom-call | tf_op jit(solution)/shard_map/jit(cholesky)/cholesky | solution.py:58
  266.6 0.7 compare_reduce_fusion
  267.3 1.3 select_bitcast_fusion.1
  269.1 2.0 fusion.14
  272.3 10.6 %custom-call.11 = f32[1,128,128]{1,2,0:T(8,128)S(1)} custom-call(f32[1,128,128]{2,1,0:T(8,128)} %get-tuple-element.31), custom_call_target="InvertDiagBlocksLowerTriangular" | custom-call | tf_op jit(solution)/shard_map/triangular_solve/custom-call.0 | solution.py:59
  285.2 3.1 slice.157
  288.3 7.0 %gather_fusion.3 = f32[1024,512]{1,0:T(8,128)} fusion(f32[1024,512]{1,0:T(8,128)} %slice.157, s32[1024]{0:T(1024)S(1)} %get-tuple-element.58), kind=kCustom, calls=%fused_computation.5 | custom fusion | bytes 4198400 | tf_op jit(solution)/shard_map/gather | solution.py:135
  295.4 5.2 %fusion.87 = f32[1024,512]{1,0:T(8,128)S(1)} fusion(f32[1024,512]{1,0:T(8,128)} %gather_fusion.4, f32[128,256]{1,0:T(8,128)S(1)} %broadcast.165, f32[128,128]{1,0:T(8,128)S(1)} %cholesky.75, f32[128,128]{1,0:T(8,128)S(1)} %fusion.30, f32[128,128]{1,0:T(8,128)S(1)} %copy.52, f32[128,128]{1,0:T(8,128)S(1)} %convolution_negate_fusion, ...), kind=kOutput, calls=%fused_computation.193 | convolution fusion | flops 3224633344 | bytes 5046272 | tf_op jit(solution)/shard_map/dot_general | solution.py:136
  300.6 3.5 fusion.89
  304.1 7.5 %select_bitcast_fusion = f32[128,8,8,128]{3,1,2,0:T(8,128)S(1)} fusion(f32[1024,1024]{1,0:T(8,128)S(1)} %copy-done.1, f32[1024,512]{1,0:T(8,128)S(1)} %fusion.89, f32[1024,512]{1,0:T(8,128)S(1)} %fusion.87, pred[1024]{0:T(1024)(128)(4,1)S(1)} %gather_fusion.2, pred[1024]{0:T(1024)(128)(4,1)S(1)} %gather_fusion.1), kind=kOutput, calls=%fused_computation.16 | convolution fusion | flops 6445596672 | bytes 12584960 | tf_op jit(solution)/shard_map/dot_general | solution.py:134
  311.6 1.0 copy.71
  312.6 2.8 copy.53
  315.4 9.2 %all-to-all-start.2 = ((f32[128,64,128]{2,1,0:T(8,128)}), f32[128,64,128]{2,1,0:T(8,128)}, u32[]{:S(2)}, u32[]{:S(2)}) async-start(f32[128,64,128]{2,1,0:T(8,128)} %bitcast.135), calls=%async_computation.2 | async-start | bytes 8388608 | tf_op jit(solution)/shard_map/all_to_all | solution.py:153
  325.4 6.8 %sort.93 = (s32[8192]{0:T(1024)}, s32[8192]{0:T(1024)S(1)}) sort(s32[8192]{0:T(1024)S(1)} %get-tuple-element.55, s32[8192]{0:T(1024)S(1)} %iota.134), dimensions={0}, to_apply=%region_6.9 | sort | flops 106496 | bytes 131072 | tf_op jit(solution)/shard_map/jit(argsort)/sort | solution.py:32
  332.1 6.1 %gather_fusion.6 = s32[1024]{0:T(1024)S(1)} fusion(s32[8192]{0:T(1024)S(1)} %bitcast.130, s32[1024]{0:T(1024)S(1)} %fusion.60), kind=kCustom, calls=%fused_computation.8 | custom fusion | bytes 12288 | tf_op jit(solution)/shard_map/gather | solution.py:33
  338.3 6.8 %sort.92 = (s32[8192]{0:T(1024)}, s32[8192]{0:T(1024)S(1)}) sort(s32[8192]{0:T(1024)S(1)} %get-tuple-element.54, s32[8192]{0:T(1024)S(1)} %iota.132), dimensions={0}, to_apply=%region_5.8 | sort | flops 106496 | bytes 131072 | tf_op jit(solution)/shard_map/jit(argsort)/sort | solution.py:32
  345.1 4.3 gather_fusion.5
  349.4 6.8 %sort.95 = (s32[8192]{0:T(1024)}, s32[8192]{0:T(1024)S(1)}) sort(s32[8192]{0:T(1024)S(1)} %get-tuple-element.52, s32[8192]{0:T(1024)S(1)} %iota.139), dimensions={0}, to_apply=%region_9.13 | sort | flops 106496 | bytes 131072 | tf_op jit(solution)/shard_map/jit(argsort)/sort | solution.py:32
  356.1 6.3 %gather_fusion.8 = s32[1024]{0:T(1024)S(1)} fusion(s32[8192]{0:T(1024)S(1)} %bitcast.127, s32[1024]{0:T(1024)S(1)} %fusion.61), kind=kCustom, calls=%fused_computation.10 | custom fusion | bytes 12288 | tf_op jit(solution)/shard_map/gather | solution.py:33
  362.5 7.6 %sort.94 = (s32[8192]{0:T(1024)}, s32[8192]{0:T(1024)}) sort(s32[8192]{0:T(1024)} %get-tuple-element.53, s32[8192]{0:T(1024)S(1)} %iota.137), dimensions={0}, to_apply=%region_8.12 | sort | flops 106496 | bytes 131072 | tf_op jit(solution)/shard_map/jit(argsort)/sort | solution.py:32
  370.8 3.1 gather_fusion.7
  374.0 4.3 scatter_custom_fusion
  378.3 4.3 scatter_custom_fusion.1
  385.2 5.9 %fusion.10 = f32[1,1024,512]{2,1,0:T(8,128)} fusion(f32[512,512]{1,0:T(8,128)S(1)} %copy-done.4, pred[1024]{0:T(1024)(128)(4,1)} %get-tuple-element.56, pred[1024]{0:T(1024)(128)(4,1)} %get-tuple-element.57, f32[1,1024,512]{2,1,0:T(8,128)S(1)} %copy-done, f32[128,256]{1,0:T(8,128)S(1)} %broadcast.165, f32[128,128]{1,0:T(8,128)} %copy-done.6, ...), kind=kOutput, calls=%fused_computation.29 | convolution fusion | flops 3225681920 | bytes 6096896 | tf_op jit(solution)/shard_map/dot_general | solution.py:89
  391.1 5.5 %copy.83 = f32[2,8,8,64,128]{4,1,3,2,0:T(8,128)S(1)} copy(f32[2,8,8,64,128]{4,3,2,1,0:T(8,128)} %bitcast.26) | data formatting | bytes 8388608 | tf_op jit(solution)/shard_map/reshape | solution.py:157
  396.9 5.4 %fusion.6 = f32[1024,768]{1,0:T(8,128)S(1)} fusion(f32[64,8,8,128]{3,2,1,0:T(8,128)S(1)} %bitcast.139, s32[512]{0:T(512)S(1)} %broadcast_subtract_fusion.3), kind=kOutput, calls=%fused_computation.24 | convolution fusion | flops 4832231424 | bytes 5244928 | tf_op jit(solution)/shard_map/qi,pq->ip/dot_general | solution.py:168
  403.1 5.2 %fusion.3 = f32[1024,768]{1,0:T(8,128)S(1)} fusion(f32[64,8,8,128]{3,2,1,0:T(8,128)S(1)} %bitcast.138, s32[512]{0:T(512)S(1)} %copy-done.16), kind=kOutput, calls=%fused_computation.21 | convolution fusion | flops 4832231424 | bytes 5244928 | tf_op jit(solution)/shard_map/qi,pq->ip/dot_general | solution.py:168
  408.3 1.9 pad.14
  410.2 5.5 %gather_fusion.9 = f32[1536,768]{1,0:T(8,128)} fusion(f32[1025,768]{1,0:T(8,128)S(1)} %pad.13, s32[2048]{0:T(1024)S(1)} %pad_clamp_fusion.1), kind=kCustom, calls=%fused_computation.clone | custom fusion | bytes 9443328 | tf_op jit(solution)/shard_map/jit(_take)/gather | solution.py:173
  415.7 8.7 %gather_fusion.10 = f32[1536,768]{1,0:T(8,128)} fusion(f32[1025,768]{1,0:T(8,128)} %pad.14, s32[2048]{0:T(1024)S(1)} %pad_clamp_fusion), kind=kCustom, calls=%fused_computation.1.clone | custom fusion | bytes 9443328 | tf_op jit(solution)/shard_map/jit(_take)/gather | solution.py:173
  424.4 8.0 %select_add_fusion = f32[1536,768]{1,0:T(8,128)} fusion(f32[1536,768]{1,0:T(8,128)} %gather_fusion.10, f32[1536,768]{1,0:T(8,128)} %param.10, f32[1536,768]{1,0:T(8,128)} %gather_fusion.9, pred[1536]{0:T(1024)(128)(4,1)S(1)} %copy-done.15, pred[1536]{0:T(1024)(128)(4,1)S(1)} %copy-done.14), kind=kLoop, calls=%fused_computation.13 | loop fusion | flops 4718592 | bytes 18877440 | tf_op jit(solution)/shard_map/add | solution.py:173
  (134 shorter events, 20.3 us)
Async XLA Ops:
  7.2 86.7 %all-gather.6.cloned.1.call-start = ((), (), s32[]{:S(2)}) async-start(), calls=%async_computation.4 | async-start | bytes 2359296 | tf_op jit(solution)/shard_map/all_gather | solution.py:26
  41.9 127.0 %all-gather.4.cloned.1.call-start = ((), (), s32[]{:S(2)}) async-start(), calls=%async_computation.3 | async-start | bytes 3538944 | tf_op jit(solution)/shard_map/all_gather | solution.py:19
  93.9 2.2 copy-start
  139.2 3.0 copy-start.17
  168.9 1.2 slice-start
  197.5 0.8 copy-start.2
  269.1 31.4 %copy-start.6 = (f32[128,128]{1,0:T(8,128)}, f32[128,128]{1,0:T(8,128)S(1)}, u32[]{:S(2)}) copy-start(f32[128,128]{1,0:T(8,128)S(1)} %cholesky.75) | copy-start | bytes 196612
  271.1 14.0 %copy-start.7 = (s32[2,8192]{1,0:T(2,128)S(1)}, s32[2,8192]{1,0:T(2,128)}, u32[]{:S(2)}) copy-start(s32[2,8192]{1,0:T(2,128)} %param.11) | copy-start | bytes 196612
  283.3 17.3 %copy-start.13 = (f32[128,128]{1,0:T(8,128)}, f32[128,128]{1,0:T(8,128)S(1)}, u32[]{:S(2)}) copy-start(f32[128,128]{1,0:T(8,128)S(1)} %copy.52) | copy-start | bytes 196612
  283.9 16.7 %copy-start.8 = (f32[128,128]{1,0:T(8,128)}, f32[128,128]{1,0:T(8,128)S(1)}, u32[]{:S(2)}) copy-start(f32[128,128]{1,0:T(8,128)S(1)} %convolution_negate_fusion.2) | copy-start | bytes 196612
  284.2 16.4 %copy-start.5 = (f32[128,128]{1,0:T(8,128)}, f32[128,128]{1,0:T(8,128)S(1)}, u32[]{:S(2)}) copy-start(f32[128,128]{1,0:T(8,128)S(1)} %convolution_negate_fusion.3) | copy-start | bytes 196612
  284.8 15.8 %copy-start.9 = (f32[128,128]{1,0:T(8,128)}, f32[128,128]{1,0:T(8,128)S(1)}, u32[]{:S(2)}) copy-start(f32[128,128]{1,0:T(8,128)S(1)} %convolution_negate_fusion.1) | copy-start | bytes 196612
  285.1 15.5 %copy-start.10 = (f32[128,128]{1,0:T(8,128)}, f32[128,128]{1,0:T(8,128)S(1)}, u32[]{:S(2)}) copy-start(f32[128,128]{1,0:T(8,128)S(1)} %convolution_negate_fusion) | copy-start | bytes 196612
  288.3 7.1 %copy-start.11 = (f32[128,128]{1,0:T(8,128)S(1)}, f32[128,128]{1,0:T(8,128)}, u32[]{:S(2)}) copy-start(f32[128,128]{1,0:T(8,128)} %copy.48) | copy-start | bytes 196612
  288.3 7.1 %copy-start.12 = (f32[128,128]{1,0:T(8,128)S(1)}, f32[128,128]{1,0:T(8,128)}, u32[]{:S(2)}) copy-start(f32[128,128]{1,0:T(8,128)} %copy.45) | copy-start | bytes 196612
  295.4 5.3 %copy-start.3 = (f32[1024,512]{1,0:T(8,128)S(1)}, f32[1024,512]{1,0:T(8,128)}, u32[]{:S(2)}) copy-start(f32[1024,512]{1,0:T(8,128)} %gather_fusion.3) | copy-start | bytes 6291460
  300.6 3.5 copy-start.1
  315.4 75.7 %all-to-all-start.2 = ((f32[128,64,128]{2,1,0:T(8,128)}), f32[128,64,128]{2,1,0:T(8,128)}, u32[]{:S(2)}, u32[]{:S(2)}) async-start(f32[128,64,128]{2,1,0:T(8,128)} %bitcast.135), calls=%async_computation.2 | async-start | bytes 8388608 | tf_op jit(solution)/shard_map/all_to_all | solution.py:153
  362.5 22.7 %copy-start.4 = (f32[512,512]{1,0:T(8,128)S(1)}, f32[512,512]{1,0:T(8,128)}, u32[]{:S(2)}) copy-start(f32[512,512]{1,0:T(8,128)} %fusion.14) | copy-start | bytes 3145732
  402.4 0.7 copy-start.16
  415.7 8.7 %copy-start.14 = (pred[1536]{0:T(1024)(128)(4,1)S(1)}, pred[1536]{0:T(1024)(128)(4,1)}, u32[]{:S(2)}) copy-start(pred[1536]{0:T(1024)(128)(4,1)} %compare_and_fusion.1) | copy-start | bytes 4612
  415.7 8.7 %copy-start.15 = (pred[1536]{0:T(1024)(128)(4,1)S(1)}, pred[1536]{0:T(1024)(128)(4,1)}, u32[]{:S(2)}) copy-start(pred[1536]{0:T(1024)(128)(4,1)} %compare_and_fusion) | copy-start | bytes 4612
Sparse Core Ops, SparseCore 0:
  42.0 51.8 all-gather.5
  142.3 26.5 all-gather.3
